TPU v7x, 32 devices: a whole 2x2x4 slice. The times are simulated.
32 devices in a mesh: dp: 4 (over z), tensor: 8 (over y, x, core).
Axes of the slice: x: 2, y: 2, z: 4, core: 2. Of those that a mesh axis runs over, the one named last changes fastest.
Arguments:
- inputs: bfloat16 [4, 32, 4096], P(None, 'tensor', 'dp'), may hold values from -6 to 6
- norm_gain: float32 [4096], P('dp'), may hold values from 0.1 to 1.9
- w_gate: bfloat16 [4096, 28672], P('dp', 'tensor'), may hold values from -0.09375 to 0.09375
- w_up: bfloat16 [4096, 28672], P('dp', 'tensor'), may hold values from -0.09375 to 0.09375
- w_down: bfloat16 [28672, 4096], P('tensor', 'dp'), may hold values from -0.03125 to 0.03125
- d_output: bfloat16 [4, 32, 4096], P(None, 'tensor', 'dp'), may hold values from -0.75 to 0.75
- level_of_batch: int32 [4], replicated, may hold values from 0 to 3, each once
Outputs:
- outputs: bfloat16 [4, 32, 4096], P(None, 'tensor', 'dp')
- d_inputs: bfloat16 [4, 32, 4096], P(None, 'tensor', 'dp')
- d_gain: float32 [4096], P('dp')
- d_gate: bfloat16 [4096, 28672], P('dp', 'tensor')
- d_up: bfloat16 [4096, 28672], P('dp', 'tensor')
- d_down: bfloat16 [28672, 4096], P('tensor', 'dp')
- row_product: float32 [4, 32], P(None, 'tensor')
Inputs may be any that keep to these rules, and one draw needn't show every extreme that they name: `level_of_batch`: every level from 0 to 3 belongs to exactly one micro-batch.
All inputs are finite; a program needn't handle non-finite values.
Results may differ from a plain program's by a relative error of at most 0.02.
Values may be sent and summed in bfloat16 or wider, within the bound.
No kernel may reach another device: no remote copies, remote signals or barrier semaphores. Data moves between devices by JAX's collectives and lax.ppermute only.
A program may use at most 384 MiB of HBM per device.

v0:
```python
import jax
import jax.numpy as jnp
from jax import lax
from jax.sharding import PartitionSpec as P

epsilon = 1e-05
contract_cols = (((1,), (1,)), ((), ()))
contract_rows = (((0,), (0,)), ((), ()))


def local_terms(gate_sum, up_sum, back_sum, active_mask):
    sigmoid_gate = jax.nn.sigmoid(gate_sum)
    silu_gate = gate_sum * sigmoid_gate
    slope = sigmoid_gate * (1.0 + gate_sum * (1.0 - sigmoid_gate))
    hidden = (silu_gate * up_sum * active_mask).astype(jnp.bfloat16)
    gate_grad = (back_sum * up_sum * slope * active_mask).astype(jnp.bfloat16)
    up_grad = (back_sum * silu_gate * active_mask).astype(jnp.bfloat16)
    return (hidden, gate_grad, up_grad)


def per_device(inputs, norm_gain, w_gate, w_up, w_down, d_output, level_of_batch):
    groups = lax.axis_size("tensor")
    tensor_index = lax.axis_index("tensor")
    local_feat = w_gate.shape[0]
    local_cols = w_gate.shape[1]
    full_width = local_feat * lax.axis_size("dp")
    batches, local_rows, _ = inputs.shape
    both = jnp.concatenate([inputs, d_output], axis=0).transpose(1, 0, 2)
    both_all = lax.all_gather(both, "tensor", axis=0, tiled=True)
    inputs_all = both_all[:, :batches].astype(jnp.float32)
    grad_all = both_all[:, batches:]
    rows = inputs_all.shape[0]
    square_sum = lax.psum(jnp.sum(inputs_all * inputs_all, axis=2), "dp")
    row_scale_all = lax.rsqrt(square_sum / full_width + epsilon)
    normed_all = (inputs_all * row_scale_all[:, :, None] * norm_gain).astype(jnp.bfloat16)
    start = tensor_index * local_rows
    row_scale = lax.dynamic_slice_in_dim(row_scale_all, start, local_rows, axis=0).T
    wide_inputs = inputs.astype(jnp.float32)
    flat_normed = normed_all.reshape(rows * batches, local_feat)
    flat_grad = grad_all.reshape(rows * batches, local_feat)
    gate_part = jnp.dot(flat_normed, w_gate, preferred_element_type=jnp.float32)
    up_part = jnp.dot(flat_normed, w_up, preferred_element_type=jnp.float32)
    back_part = lax.dot_general(
        flat_grad, w_down, contract_cols, preferred_element_type=jnp.float32
    )
    gate_sum, up_sum, back_sum = (
        lax.psum(gate_part.astype(jnp.bfloat16), "dp").astype(jnp.float32),
        lax.psum(up_part.astype(jnp.bfloat16), "dp").astype(jnp.float32),
        lax.psum(back_part.astype(jnp.bfloat16), "dp").astype(jnp.float32),
    )
    halvings = 3 - level_of_batch
    active = (tensor_index < jnp.right_shift(groups, halvings)).astype(jnp.float32)
    active_mask = jnp.tile(active, rows)[:, None]
    hidden, gate_grad, up_grad = local_terms(gate_sum, up_sum, back_sum, active_mask)
    down_part = jnp.dot(hidden, w_down, preferred_element_type=jnp.float32)
    normed_part = lax.dot_general(
        gate_grad, w_gate, contract_cols, preferred_element_type=jnp.float32
    ) + lax.dot_general(up_grad, w_up, contract_cols, preferred_element_type=jnp.float32)
    stacked = jnp.stack(
        [
            down_part.reshape(rows, batches, local_feat),
            normed_part.reshape(rows, batches, local_feat),
        ],
        axis=1,
    ).astype(jnp.bfloat16)
    stacked = stacked.reshape(rows, 2 * batches, local_feat)
    shares = lax.psum_scatter(stacked, "tensor", scatter_dimension=0, tiled=True).astype(
        jnp.float32
    )
    shares = shares.reshape(local_rows, 2, batches, local_feat)
    down_output = shares[:, 0].transpose(1, 0, 2)
    normed_grad = shares[:, 1].transpose(1, 0, 2)
    down_out = lax.dot_general(
        hidden, flat_grad, contract_rows, preferred_element_type=jnp.float32
    ).astype(jnp.bfloat16)
    gate_out = lax.dot_general(
        flat_normed, gate_grad, contract_rows, preferred_element_type=jnp.float32
    ).astype(jnp.bfloat16)
    up_out = lax.dot_general(
        flat_normed, up_grad, contract_rows, preferred_element_type=jnp.float32
    ).astype(jnp.bfloat16)
    wide_grad = d_output.astype(jnp.float32)
    weighted = norm_gain * normed_grad
    row_part = jnp.sum(weighted * wide_inputs, axis=2)
    gain_part = jnp.sum(normed_grad * wide_inputs * row_scale[:, :, None], axis=(0, 1))
    dp_index = lax.axis_index("dp")
    row_slots = jnp.zeros((groups,) + row_part.shape, jnp.float32)
    row_slots = lax.dynamic_update_index_in_dim(row_slots, row_part, tensor_index, 0)
    gain_slots = jnp.zeros((lax.axis_size("dp"), local_feat), jnp.float32)
    gain_slots = lax.dynamic_update_index_in_dim(gain_slots, gain_part, dp_index, 0)
    row_slots, gain_slots = lax.psum((row_slots, gain_slots), ("dp", "tensor"))
    row_product = lax.dynamic_index_in_dim(row_slots, tensor_index, 0, keepdims=False)
    d_gain = lax.dynamic_index_in_dim(gain_slots, dp_index, 0, keepdims=False)
    outputs = (wide_inputs + down_output).astype(jnp.bfloat16)
    scale_cube = row_scale * row_scale * row_scale
    d_inputs = (
        wide_grad
        + row_scale[:, :, None] * weighted
        - wide_inputs * (scale_cube * row_product / full_width)[:, :, None]
    ).astype(jnp.bfloat16)
    return (outputs, d_inputs, d_gain, gate_out, up_out, down_out, row_product)


def solution(mesh):
    in_specs = (
        P(None, "tensor", "dp"),
        P("dp"),
        P("dp", "tensor"),
        P("dp", "tensor"),
        P("tensor", "dp"),
        P(None, "tensor", "dp"),
        P(),
    )
    out_specs = (
        P(None, "tensor", "dp"),
        P(None, "tensor", "dp"),
        P("dp"),
        P("dp", "tensor"),
        P("dp", "tensor"),
        P("tensor", "dp"),
        P(None, "tensor"),
    )
    return jax.shard_map(
        per_device, mesh=mesh, in_specs=in_specs, out_specs=out_specs, check_vma=False
    )
```

profile of v0, /device:TPU:0, one launch (start us, length us, event | category | flops | bytes accessed | tf_op | source)
XLA Modules:
  0.0 270.4 jit_solution(21029129249374350)
XLA Ops:
  7.2 0.8 copy.27
  8.0 0.8 copy.26
  8.8 11.3 %all_gather.3 = bf16[32,8,1024]{2,1,0:T(8,128)(2,1)S(1)} all-gather(bf16[4,8,1024]{2,1,0:T(8,128)(2,1)S(1)} %maximum_bitcast_fusion), channel_id=1, replica_groups=mesh['dp'=4,'tensor'=8] {'tensor'}, dimensions={0}, use_global_device_ids=true | all-gather | bytes 589824 | tf_op jit(solution)/shard_map/all_gather | solution.py:29
  20.2 0.2 fusion.13
  20.4 0.8 slice.17
  21.2 19.0 %psum.42 = f32[32,4]{1,0:T(8,128)S(1)} all-reduce(f32[32,4]{1,0:T(8,128)S(1)} %fusion.13), channel_id=1, replica_groups=mesh['dp'=4,'tensor'=8] {'dp'}, use_global_device_ids=true, to_apply=%region_1.0 | all-reduce | flops 128 | bytes 1024 | tf_op jit(solution)/shard_map/psum | solution.py:33
  40.2 0.9 fusion.15
  41.2 1.9 reshape.36
  43.1 5.3 %convolution_convert_fusion.4 = bf16[128,3584]{1,0:T(8,128)(2,1)} fusion(bf16[128,1024]{1,0:T(8,128)(2,1)S(1)} %reshape.35, bf16[1024,3584]{1,0:T(8,128)(2,1)} %param.10), kind=kOutput, calls=%fused_computation.4 | convolution fusion | flops 939982848 | bytes 8519680 | tf_op jit(solution)/shard_map/dot_general | solution.py:42
  48.4 2.1 convolution_convert_fusion.5
  50.5 3.5 %convolution_convert_fusion.3 = bf16[128,3584]{1,0:T(8,128)(2,1)} fusion(bf16[128,1024]{1,0:T(8,128)(2,1)S(1)} %copy-done, bf16[3584,1024]{1,0:T(8,128)(2,1)S(1)} %bitcast.49), kind=kOutput, calls=%fused_computation.3 | convolution fusion | flops 939982848 | bytes 8519680 | tf_op jit(solution)/shard_map/dot_general | solution.py:43
  53.9 0.2 reduce-scatter.2.cloned.1.call-start
  54.2 0.4 copy-done.13
  54.6 0.1 mul.117
  54.8 104.9 %all-reduce.4.cloned.1.call-done = (bf16[128,3584]{1,0:T(8,128)(2,1)}, bf16[128,3584]{1,0:T(8,128)(2,1)}, bf16[128,3584]{1,0:T(8,128)(2,1)}) async-done(((bf16[128,3584]{1,0:T(8,128)(2,1)}, bf16[128,3584]{1,0:T(8,128)(2,1)}, bf16[128,3584]{1,0:T(8,128)(2,1)}), (bf16[128,3584]{1,0:T(8,128)(2,1)}, bf16[128,3584]{1,0:T(8,128)(2,1)}, bf16[128,3584]{1,0:T(8,128)(2,1)})) %all-reduce.4.cloned.1.call-update) | async-done | bytes 2752528 | tf_op jit(solution)/shard_map/psum | solution.py:48
  159.7 5.9 %convolution_convert_fusion.6 = bf16[128,1024]{1,0:T(8,128)(2,1)} fusion(bf16[3584,1024]{1,0:T(8,128)(2,1)} %param.11, bf16[128,3584]{1,0:T(8,128)(2,1)} %get-tuple-element.11, f32[128]{0:T(128)S(1)} %mul.117, bf16[128,3584]{1,0:T(8,128)(2,1)} %get-tuple-element.13), kind=kOutput, calls=%fused_computation.26 | convolution fusion | flops 943783936 | bytes 9437696 | tf_op jit(solution)/shard_map/dot_general | solution.py:55
  165.7 5.4 %convolution_convert_fusion = bf16[3584,1024]{1,0:T(8,128)(2,1)} fusion(bf16[128,1024]{1,0:T(8,128)(2,1)S(1)} %copy-done.1, bf16[128,3584]{1,0:T(8,128)(2,1)S(1)} %copy-done.6, f32[128]{0:T(128)S(1)} %mul.117, bf16[128,3584]{1,0:T(8,128)(2,1)S(1)} %copy-done.10), kind=kOutput, calls=%fused_computation | convolution fusion | flops 947322880 | bytes 9437696 | tf_op jit(solution)/shard_map/dot_general | solution.py:73
  171.1 1.9 stack_reshape.8
  173.0 1.7 copy.28
  174.7 6.6 %fusion.30 = f32[128,1024]{1,0:T(8,128)S(1)} fusion(bf16[1024,3584]{1,0:T(8,128)(2,1)} %param.9, bf16[128,3584]{1,0:T(8,128)(2,1)} %get-tuple-element.11, bf16[128,3584]{1,0:T(8,128)(2,1)} %get-tuple-element.12, bf16[128,3584]{1,0:T(8,128)(2,1)} %get-tuple-element.13, f32[128]{0:T(128)S(1)} %mul.117), kind=kOutput, calls=%fused_computation.56 | convolution fusion | flops 945946624 | bytes 10617344 | tf_op jit(solution)/shard_map/dot_general | solution.py:56
  181.4 3.3 %fusion.12 = bf16[128,1024]{1,0:T(8,128)(2,1)} fusion(f32[128,1024]{1,0:T(8,128)S(1)} %fusion.30, bf16[1024,3584]{1,0:T(8,128)(2,1)S(1)} %bitcast.47, bf16[128,3584]{1,0:T(8,128)(2,1)S(1)} %copy-done.8, f32[128]{0:T(128)S(1)} %mul.117, bf16[128,3584]{1,0:T(8,128)(2,1)S(1)} %copy-done.11), kind=kOutput, calls=%fused_computation.25 | convolution fusion | flops 943915008 | bytes 9961984 | tf_op jit(solution)/shard_map/dot_general | solution.py:58
  184.7 1.2 stack_reshape.9
  186.0 1.0 pad_maximum_fusion
  187.0 1.1 copy.30
  188.1 5.4 %convolution_convert_fusion.1 = bf16[1024,3584]{1,0:T(8,128)(2,1)} fusion(bf16[128,1024]{1,0:T(8,128)(2,1)S(1)} %reshape.35, bf16[128,3584]{1,0:T(8,128)(2,1)S(1)} %copy-done.9, f32[128]{0:T(128)S(1)} %mul.117, bf16[128,3584]{1,0:T(8,128)(2,1)S(1)} %copy-done.12), kind=kOutput, calls=%fused_computation.1 | convolution fusion | flops 947322880 | bytes 9437696 | tf_op jit(solution)/shard_map/dot_general | solution.py:79
  193.5 5.4 %convolution_convert_fusion.2 = bf16[1024,3584]{1,0:T(8,128)(2,1)} fusion(bf16[128,1024]{1,0:T(8,128)(2,1)S(1)} %reshape.35, bf16[128,3584]{1,0:T(8,128)(2,1)S(1)} %copy-done.7, bf16[128,3584]{1,0:T(8,128)(2,1)S(1)} %copy-done.9, bf16[128,3584]{1,0:T(8,128)(2,1)S(1)} %copy-done.12, f32[128]{0:T(128)S(1)} %mul.117), kind=kOutput, calls=%fused_computation.2 | convolution fusion | flops 949616640 | bytes 10355200 | tf_op jit(solution)/shard_map/dot_general | solution.py:76
  198.9 22.4 %reduce-scatter.2.cloned.1.call-done = bf16[4,8,1024]{2,1,0:T(8,128)(2,1)} async-done(((bf16[32,8,1024]{2,1,0:T(8,128)(2,1)}), bf16[4,8,1024]{2,1,0:T(8,128)(2,1)}) %reduce-scatter.2.cloned.1.call-update) | async-done | bytes 65552 | tf_op jit(solution)/shard_map/reduce_scatter | solution.py:67
  221.4 0.9 copy.36
  222.3 0.1 fusion.21
  222.5 39.5 %all-reduce = (f32[8,4,4]{2,1,0:T(4,128)S(1)}, f32[4,1024]{1,0:T(4,128)S(1)}) all-reduce(f32[8,4,4]{2,1,0:T(4,128)S(1)} %bitcast_dynamic-update-slice_fusion, f32[4,1024]{1,0:T(4,128)S(1)} %dynamic_update_slice.9), channel_id=1, replica_groups=mesh['dp'=4,'tensor'=8] {'dp','tensor'}, use_global_device_ids=true, to_apply=%region_7.0 | all-reduce | flops 4224 | bytes 33792 | tf_op jit(solution)/shard_map/psum | solution.py:91
  262.3 0.7 fusion.19
  263.0 0.6 constant_dynamic-slice_fusion
  (61 shorter events, 0.8 us)
Async XLA Ops:
  7.2 152.6 %all-reduce.4.cloned.1.call-start = ((), (), s32[]{:S(2)}) async-start(), calls=%async_computation.2 | async-start | bytes 5505024 | tf_op jit(solution)/shard_map/psum | solution.py:48
  41.2 7.2 %slice-start = ((s8[7340032]{0:T(1024)(128)(4,1)}), s8[3145728]{0:T(1024)(128)(4,1)S(1)}, s32[]{:S(2)}) async-start(s8[7340032]{0:T(1024)(128)(4,1)} %bitcast.44), calls=%async_computation.3 | async-start | bytes 6291456
  43.1 5.3 %slice-start.1 = ((s8[7340032]{0:T(1024)(128)(4,1)}), s8[4194304]{0:T(1024)(128)(4,1)S(1)}, s32[]{:S(2)}) async-start(s8[7340032]{0:T(1024)(128)(4,1)} %bitcast.44), calls=%async_computation.4 | async-start | bytes 8388608
  43.1 7.4 %slice-start.4 = ((s8[7340032]{0:T(1024)(128)(4,1)}), s8[4194304]{0:T(1024)(128)(4,1)S(1)}, s32[]{:S(2)}) async-start(s8[7340032]{0:T(1024)(128)(4,1)} %bitcast.48), calls=%async_computation.7 | async-start | bytes 8388608
  48.4 2.1 slice-start.5
  48.4 2.1 copy-start
  53.9 0.7 copy-start.13
  53.9 167.4 %reduce-scatter.2.cloned.1.call-start = ((), (), s32[]{:S(2)}) async-start(), calls=%async_computation.1 | async-start | bytes 589824 | tf_op jit(solution)/shard_map/reduce_scatter | solution.py:67
  159.7 5.9 %copy-start.1 = (bf16[128,1024]{1,0:T(8,128)(2,1)S(1)}, bf16[128,1024]{1,0:T(8,128)(2,1)}, u32[]{:S(2)}) copy-start(bf16[128,1024]{1,0:T(8,128)(2,1)} %reshape.36) | copy-start | bytes 786436
  159.7 5.9 %copy-start.6 = (bf16[128,3584]{1,0:T(8,128)(2,1)S(1)}, bf16[128,3584]{1,0:T(8,128)(2,1)}, u32[]{:S(2)}) copy-start(bf16[128,3584]{1,0:T(8,128)(2,1)} %get-tuple-element.11) | copy-start | bytes 2752516
  159.7 5.9 %copy-start.10 = (bf16[128,3584]{1,0:T(8,128)(2,1)S(1)}, bf16[128,3584]{1,0:T(8,128)(2,1)}, u32[]{:S(2)}) copy-start(bf16[128,3584]{1,0:T(8,128)(2,1)} %get-tuple-element.13) | copy-start | bytes 2752516
  171.1 10.3 %slice-start.2 = ((s8[7340032]{0:T(1024)(128)(4,1)}), s8[3145728]{0:T(1024)(128)(4,1)S(1)}, s32[]{:S(2)}) async-start(s8[7340032]{0:T(1024)(128)(4,1)} %bitcast.46), calls=%async_computation.5 | async-start | bytes 6291456
  174.7 6.6 %slice-start.3 = ((s8[7340032]{0:T(1024)(128)(4,1)}), s8[4194304]{0:T(1024)(128)(4,1)S(1)}, s32[]{:S(2)}) async-start(s8[7340032]{0:T(1024)(128)(4,1)} %bitcast.46), calls=%async_computation.6 | async-start | bytes 8388608
  174.7 6.6 %copy-start.8 = (bf16[128,3584]{1,0:T(8,128)(2,1)S(1)}, bf16[128,3584]{1,0:T(8,128)(2,1)}, u32[]{:S(2)}) copy-start(bf16[128,3584]{1,0:T(8,128)(2,1)} %get-tuple-element.12) | copy-start | bytes 2752516
  174.7 6.6 %copy-start.11 = (bf16[128,3584]{1,0:T(8,128)(2,1)S(1)}, bf16[128,3584]{1,0:T(8,128)(2,1)}, u32[]{:S(2)}) copy-start(bf16[128,3584]{1,0:T(8,128)(2,1)} %get-tuple-element.13) | copy-start | bytes 2752516
  184.7 3.4 %copy-start.9 = (bf16[128,3584]{1,0:T(8,128)(2,1)S(1)}, bf16[128,3584]{1,0:T(8,128)(2,1)}, u32[]{:S(2)}) copy-start(bf16[128,3584]{1,0:T(8,128)(2,1)} %get-tuple-element.12) | copy-start | bytes 2752516
  184.7 3.4 %copy-start.12 = (bf16[128,3584]{1,0:T(8,128)(2,1)S(1)}, bf16[128,3584]{1,0:T(8,128)(2,1)}, u32[]{:S(2)}) copy-start(bf16[128,3584]{1,0:T(8,128)(2,1)} %get-tuple-element.13) | copy-start | bytes 2752516
  188.1 5.4 %copy-start.7 = (bf16[128,3584]{1,0:T(8,128)(2,1)S(1)}, bf16[128,3584]{1,0:T(8,128)(2,1)}, u32[]{:S(2)}) copy-start(bf16[128,3584]{1,0:T(8,128)(2,1)} %get-tuple-element.11) | copy-start | bytes 2752516
  193.5 28.8 %copy-start.2 = (bf16[4,4,1024]{2,1,0:T(4,128)(2,1)S(1)}, bf16[4,4,1024]{2,1,0:T(4,128)(2,1)}, u32[]{:S(2)}) copy-start(bf16[4,4,1024]{2,1,0:T(4,128)(2,1)} %param.7) | copy-start | bytes 98308
  193.5 28.8 %copy-start.4 = (f32[1024]{0:T(1024)S(1)}, f32[1024]{0:T(1024)}, u32[]{:S(2)}) copy-start(f32[1024]{0:T(1024)} %param.8) | copy-start | bytes 12292
  193.5 68.8 %copy-start.3 = (bf16[4,4,1024]{2,1,0:T(4,128)(2,1)S(1)}, bf16[4,4,1024]{2,1,0:T(4,128)(2,1)}, u32[]{:S(2)}) copy-start(bf16[4,4,1024]{2,1,0:T(4,128)(2,1)} %param.12) | copy-start | bytes 98308
  262.1 1.5 copy-start.5
Sparse Core Ops, SparseCore 0:
  54.1 105.6 all-reduce.3
  188.2 33.1 reduce-scatter.1
where the time goes:
time: 271 us; the launch traced here: 270 us
  waiting for transfers between devices  127 us (47%)
  blocking collectives  69.8 us (26%)
  matrix products  42.8 us (16%)
  between operations  14.3 us (5%)
  local copies, waits for them, and re-layouts  12.8 us (5%)
  other arithmetic  3 us (1%)
    psum x1, waiting for transfers between devices, per_device(): lax.psum(up_part.astype(jnp.bfloat16), 'dp').astype(jnp.float32)  105 us
    psum x1, blocking collectives, per_device(): row_slots, gain_slots = lax.psum((row_slots, gain_slots), ('dp', 'tensor'))  39.5 us
    reduce_scatter x1, waiting for transfers between devices, per_device(): lax.psum_scatter(stacked, 'tensor', scatter_dimension=0, tiled=True)  22.4 us
    psum x1, blocking collectives, per_device(): square_sum = lax.psum(jnp.sum(inputs_all * inputs_all, axis=2), 'dp')  19 us
    all_gather x1, blocking collectives, per_device(): both_all = lax.all_gather(both, 'tensor', axis=0, tiled=True)  11.3 us
    dot_general x1, matrix products, per_device(): lax.dot_general(gate_grad, w_gate, contract_cols, preferred_element_type=...  6.6 us
    dot_general x1, matrix products, per_device(): down_part = jnp.dot(hidden, w_down, preferred_element_type=jnp.float32)  5.93 us
    dot_general x1, matrix products, per_device(): lax.dot_general(flat_normed, gate_grad, contract_rows, preferred_element_...  5.43 us
  transfers between devices with their start and end apart: 2, of which 2 were waited for; matrix products, arithmetic and copies ran while one was open for 4% of the time, Pallas kernels for 0%

commit v1 on v0

--- a/solution.py
+++ b/solution.py
@@ -26,7 +26,25 @@
     full_width = local_feat * lax.axis_size("dp")
     batches, local_rows, _ = inputs.shape
     both = jnp.concatenate([inputs, d_output], axis=0).transpose(1, 0, 2)
-    both_all = lax.all_gather(both, "tensor", axis=0, tiled=True)
+    tmp = jax.lax.axis_size("tensor")
+    e_now = jax.lax.axis_index("tensor")
+    o_now, h_now, f_now = (tmp, e_now, both.shape[0])
+    fields = [rr * o_now if ii == 0 else rr for ii, rr in enumerate(both.shape)]
+    p_next = jnp.zeros(fields, both.dtype)
+    both_all = lax.dynamic_update_slice_in_dim(p_next, both, h_now * f_now, axis=0)
+    val = piece_next = both
+    for s in range(1, o_now // 2 + 1):
+        val = jax.lax.ppermute(val, "tensor", [(ii, (ii + 1) % o_now) for ii in range(o_now)])
+        both_all = lax.dynamic_update_slice_in_dim(
+            both_all, val, (h_now - s) % o_now * f_now, axis=0
+        )
+        if 2 * s < o_now:
+            piece_next = jax.lax.ppermute(
+                piece_next, "tensor", [(ii, (ii - 1) % o_now) for ii in range(o_now)]
+            )
+            both_all = lax.dynamic_update_slice_in_dim(
+                both_all, piece_next, (h_now + s) % o_now * f_now, axis=0
+            )
     inputs_all = both_all[:, :batches].astype(jnp.float32)
     grad_all = both_all[:, batches:]
     rows = inputs_all.shape[0]

time: 271 us -> 280 us (1.033)
  waiting for transfers between devices: 127 us -> 140 us
  blocking collectives: 69.8 us -> 58.5 us
  starting transfers between devices: 0.26 us -> 9.05 us
    ppermute x0 -> x7, waiting for transfers between devices: none -> 12.6 us  [the longest x4 9.04 us: per_device(): jax.lax.ppermute(val, 'tensor', [(ii, (ii + 1) % o_now) for ii in range(o...]
    all_gather x1 -> x0, blocking collectives: 11.3 us -> none  [per_device(): both_all = lax.all_gather(both, 'tensor', axis=0, tiled=True)]
    ppermute x0 -> x7, starting transfers between devices: none -> 8.79 us  [the longest x3 8.78 us: per_device(): jax.lax.ppermute(piece_next, 'tensor', [(ii, (ii - 1) % o_now) for ii in...]
  transfers between devices with their start and end apart: 2 -> 9, of which waited for: 2 -> 6; matrix products, arithmetic and copies ran while one was open for 4% -> 4% of each run, Pallas kernels for 0% -> 0%
where the time goes in v1:
time: 280 us; the launch traced here: 279 us
  waiting for transfers between devices  140 us (50%)
  blocking collectives  58.5 us (21%)
  matrix products  42.8 us (15%)
  between operations  14.5 us (5%)
  local copies, waits for them, and re-layouts  11.5 us (4%)
  starting transfers between devices  9.05 us (3%)
  other arithmetic  3.1 us (1%)
    psum x1, waiting for transfers between devices, per_device(): lax.psum(up_part.astype(jnp.bfloat16), 'dp').astype(jnp.float32)  105 us
    psum x1, blocking collectives, per_device(): row_slots, gain_slots = lax.psum((row_slots, gain_slots), ('dp', 'tensor'))  39.5 us
    reduce_scatter x1, waiting for transfers between devices, per_device(): lax.psum_scatter(stacked, 'tensor', scatter_dimension=0, tiled=True)  22.5 us
    psum x1, blocking collectives, per_device(): square_sum = lax.psum(jnp.sum(inputs_all * inputs_all, axis=2), 'dp')  19 us
    ppermute x4, waiting for transfers between devices, per_device(): jax.lax.ppermute(val, 'tensor', [(ii, (ii + 1) % o_now) for ii in range(o...  9.04 us
    ppermute x3, starting transfers between devices, per_device(): jax.lax.ppermute(piece_next, 'tensor', [(ii, (ii - 1) % o_now) for ii in...  8.78 us
    dot_general x1, matrix products, per_device(): lax.dot_general(gate_grad, w_gate, contract_cols, preferred_element_type=...  6.6 us
    dot_general x1, matrix products, per_device(): down_part = jnp.dot(hidden, w_down, preferred_element_type=jnp.float32)  5.93 us
  transfers between devices with their start and end apart: 9, of which 6 were waited for; matrix products, arithmetic and copies ran while one was open for 4% of the time, Pallas kernels for 0%

profile of v1, /device:TPU:0, one launch (start us, length us, event | category | flops | bytes accessed | tf_op | source)
XLA Modules:
  0.0 279.3 jit_solution(267809807168471792)
XLA Ops:
  7.2 0.8 maximum_bitcast_fusion
  8.0 3.4 %collective-permute-start.1 = (bf16[4,8,1024]{2,0,1:T(4,128)(2,1)S(1)}, bf16[4,8,1024]{2,0,1:T(4,128)(2,1)S(1)}, u32[]{:S(2)}, u32[]{:S(2)}) collective-permute-start(bf16[4,8,1024]{2,0,1:T(4,128)(2,1)S(1)} %maximum_bitcast_fusion), channel_id=1, source_target_pairs={{0,7},{1,0},{2,1},{3,2},{4,3},{5,4},{6,5},{7,6},{8,15},{9,8},{10,9... | collective-permute-start | bytes 196616 | tf_op jit(solution)/shard_map/ppermute | solution.py:42
  11.7 1.7 collective-permute-done.1
  13.4 2.7 collective-permute-start.3
  16.1 1.8 collective-permute-done.3
  18.0 2.7 collective-permute-start.5
  20.7 4.5 %collective-permute-done.4 = bf16[4,8,1024]{2,0,1:T(4,128)(2,1)S(1)} collective-permute-done((bf16[4,8,1024]{2,0,1:T(4,128)(2,1)S(1)}, bf16[4,8,1024]{2,0,1:T(4,128)(2,1)S(1)}, u32[]{:S(2)}, u32[]{:S(2)}) %collective-permute-start.4) | collective-permute-done | bytes 65568 | tf_op jit(solution)/shard_map/ppermute | solution.py:37
  25.3 4.5 %collective-permute-done.6 = bf16[4,8,1024]{2,0,1:T(4,128)(2,1)S(1)} collective-permute-done((bf16[4,8,1024]{2,0,1:T(4,128)(2,1)S(1)}, bf16[4,8,1024]{2,0,1:T(4,128)(2,1)S(1)}, u32[]{:S(2)}, u32[]{:S(2)}) %collective-permute-start.6) | collective-permute-done | bytes 65568 | tf_op jit(solution)/shard_map/ppermute | solution.py:37
  30.1 0.8 slice.17
  30.9 19.0 %psum.42 = f32[32,4]{1,0:T(8,128)S(1)} all-reduce(f32[32,4]{1,0:T(8,128)S(1)} %fusion.13), channel_id=1, replica_groups=mesh['dp'=4,'tensor'=8] {'dp'}, use_global_device_ids=true, to_apply=%region_1.2 | all-reduce | flops 128 | bytes 1024 | tf_op jit(solution)/shard_map/psum | solution.py:51
  50.2 1.9 reshape.36
  52.1 5.3 %convolution_convert_fusion.4 = bf16[128,3584]{1,0:T(8,128)(2,1)} fusion(bf16[128,1024]{1,0:T(8,128)(2,1)S(1)} %reshape.35, bf16[1024,3584]{1,0:T(8,128)(2,1)} %param.10), kind=kOutput, calls=%fused_computation.4 | convolution fusion | flops 939982848 | bytes 8519680 | tf_op jit(solution)/shard_map/dot_general | solution.py:60
  57.4 2.1 convolution_convert_fusion.5
  59.5 3.5 %convolution_convert_fusion.3 = bf16[128,3584]{1,0:T(8,128)(2,1)} fusion(bf16[128,1024]{1,0:T(8,128)(2,1)S(1)} %copy-done, bf16[3584,1024]{1,0:T(8,128)(2,1)S(1)} %bitcast.49), kind=kOutput, calls=%fused_computation.3 | convolution fusion | flops 939982848 | bytes 8519680 | tf_op jit(solution)/shard_map/dot_general | solution.py:61
  63.2 0.4 copy-done.13
  63.8 104.8 %all-reduce.4.cloned.1.call-done = (bf16[128,3584]{1,0:T(8,128)(2,1)}, bf16[128,3584]{1,0:T(8,128)(2,1)}, bf16[128,3584]{1,0:T(8,128)(2,1)}) async-done(((bf16[128,3584]{1,0:T(8,128)(2,1)}, bf16[128,3584]{1,0:T(8,128)(2,1)}, bf16[128,3584]{1,0:T(8,128)(2,1)}), (bf16[128,3584]{1,0:T(8,128)(2,1)}, bf16[128,3584]{1,0:T(8,128)(2,1)}, bf16[128,3584]{1,0:T(8,128)(2,1)})) %all-reduce.4.cloned.1.call-update) | async-done | bytes 2752528 | tf_op jit(solution)/shard_map/psum | solution.py:66
  168.6 5.9 %convolution_convert_fusion.6 = bf16[128,1024]{1,0:T(8,128)(2,1)} fusion(bf16[3584,1024]{1,0:T(8,128)(2,1)} %param.11, bf16[128,3584]{1,0:T(8,128)(2,1)} %get-tuple-element.11, f32[128]{0:T(128)S(1)} %mul.147, bf16[128,3584]{1,0:T(8,128)(2,1)} %get-tuple-element.13), kind=kOutput, calls=%fused_computation.26 | convolution fusion | flops 943783936 | bytes 9437696 | tf_op jit(solution)/shard_map/dot_general | solution.py:73
  174.6 5.4 %convolution_convert_fusion = bf16[3584,1024]{1,0:T(8,128)(2,1)} fusion(bf16[128,1024]{1,0:T(8,128)(2,1)S(1)} %copy-done.1, bf16[128,3584]{1,0:T(8,128)(2,1)S(1)} %copy-done.6, f32[128]{0:T(128)S(1)} %mul.147, bf16[128,3584]{1,0:T(8,128)(2,1)S(1)} %copy-done.10), kind=kOutput, calls=%fused_computation | convolution fusion | flops 947322880 | bytes 9437696 | tf_op jit(solution)/shard_map/dot_general | solution.py:91
  180.0 1.9 stack_reshape.8
  181.9 1.7 copy.33
  183.7 6.6 %fusion.32 = f32[128,1024]{1,0:T(8,128)S(1)} fusion(bf16[1024,3584]{1,0:T(8,128)(2,1)} %param.9, bf16[128,3584]{1,0:T(8,128)(2,1)} %get-tuple-element.11, bf16[128,3584]{1,0:T(8,128)(2,1)} %get-tuple-element.12, bf16[128,3584]{1,0:T(8,128)(2,1)} %get-tuple-element.13, f32[128]{0:T(128)S(1)} %mul.147), kind=kOutput, calls=%fused_computation.66 | convolution fusion | flops 945946624 | bytes 10617344 | tf_op jit(solution)/shard_map/dot_general | solution.py:74
  190.3 3.3 %fusion.12 = bf16[128,1024]{1,0:T(8,128)(2,1)} fusion(f32[128,1024]{1,0:T(8,128)S(1)} %fusion.32, bf16[1024,3584]{1,0:T(8,128)(2,1)S(1)} %bitcast.47, bf16[128,3584]{1,0:T(8,128)(2,1)S(1)} %copy-done.8, f32[128]{0:T(128)S(1)} %mul.147, bf16[128,3584]{1,0:T(8,128)(2,1)S(1)} %copy-done.11), kind=kOutput, calls=%fused_computation.25 | convolution fusion | flops 943915008 | bytes 9961984 | tf_op jit(solution)/shard_map/dot_general | solution.py:76
  193.6 1.2 stack_reshape.9
  194.9 1.0 pad_maximum_fusion
  195.9 1.1 copy.35
  197.0 5.4 %convolution_convert_fusion.1 = bf16[1024,3584]{1,0:T(8,128)(2,1)} fusion(bf16[128,1024]{1,0:T(8,128)(2,1)S(1)} %reshape.35, bf16[128,3584]{1,0:T(8,128)(2,1)S(1)} %copy-done.9, f32[128]{0:T(128)S(1)} %mul.147, bf16[128,3584]{1,0:T(8,128)(2,1)S(1)} %copy-done.12), kind=kOutput, calls=%fused_computation.1 | convolution fusion | flops 947322880 | bytes 9437696 | tf_op jit(solution)/shard_map/dot_general | solution.py:97
  202.4 5.4 %convolution_convert_fusion.2 = bf16[1024,3584]{1,0:T(8,128)(2,1)} fusion(bf16[128,1024]{1,0:T(8,128)(2,1)S(1)} %reshape.35, bf16[128,3584]{1,0:T(8,128)(2,1)S(1)} %copy-done.7, bf16[128,3584]{1,0:T(8,128)(2,1)S(1)} %copy-done.9, bf16[128,3584]{1,0:T(8,128)(2,1)S(1)} %copy-done.12, f32[128]{0:T(128)S(1)} %mul.147), kind=kOutput, calls=%fused_computation.2 | convolution fusion | flops 949616640 | bytes 10355200 | tf_op jit(solution)/shard_map/dot_general | solution.py:94
  207.8 22.5 %reduce-scatter.2.cloned.1.call-done = bf16[4,8,1024]{2,1,0:T(8,128)(2,1)} async-done(((bf16[32,8,1024]{2,1,0:T(8,128)(2,1)}), bf16[4,8,1024]{2,1,0:T(8,128)(2,1)}) %reduce-scatter.2.cloned.1.call-update) | async-done | bytes 65552 | tf_op jit(solution)/shard_map/reduce_scatter | solution.py:85
  230.3 0.9 copy.41
  231.4 39.5 %all-reduce = (f32[8,4,4]{2,1,0:T(4,128)S(1)}, f32[4,1024]{1,0:T(4,128)S(1)}) all-reduce(f32[8,4,4]{2,1,0:T(4,128)S(1)} %constant_dynamic-update-slice_fusion, f32[4,1024]{1,0:T(4,128)S(1)} %dynamic_update_slice.41), channel_id=1, replica_groups=mesh['dp'=4,'tensor'=8] {'dp','tensor'}, use_global_device_ids=true, to_apply=%region_7.8 | all-reduce | flops 4224 | bytes 33792 | tf_op jit(solution)/shard_map/psum | solution.py:109
  271.2 0.7 fusion.19
  271.9 0.6 constant_dynamic-slice_fusion
  (81 shorter events, 1.9 us)
Async XLA Ops:
  7.2 42.7 %copy-start.4 = (f32[1024]{0:T(1024)S(1)}, f32[1024]{0:T(1024)}, u32[]{:S(2)}) copy-start(f32[1024]{0:T(1024)} %param.8) | copy-start | bytes 12292
  7.2 161.5 %all-reduce.4.cloned.1.call-start = ((), (), s32[]{:S(2)}) async-start(), calls=%async_computation.2 | async-start | bytes 5505024 | tf_op jit(solution)/shard_map/psum | solution.py:66
  8.0 5.3 %collective-permute-start.1 = (bf16[4,8,1024]{2,0,1:T(4,128)(2,1)S(1)}, bf16[4,8,1024]{2,0,1:T(4,128)(2,1)S(1)}, u32[]{:S(2)}, u32[]{:S(2)}) collective-permute-start(bf16[4,8,1024]{2,0,1:T(4,128)(2,1)S(1)} %maximum_bitcast_fusion), channel_id=1, source_target_pairs={{0,7},{1,0},{2,1},{3,2},{4,3},{5,4},{6,5},{7,6},{8,15},{9,8},{10,9... | collective-permute-start | bytes 196616 | tf_op jit(solution)/shard_map/ppermute | solution.py:42
  11.5 4.6 %collective-permute-start = (bf16[4,8,1024]{2,0,1:T(4,128)(2,1)S(1)}, bf16[4,8,1024]{2,0,1:T(4,128)(2,1)S(1)}, u32[]{:S(2)}, u32[]{:S(2)}) collective-permute-start(bf16[4,8,1024]{2,0,1:T(4,128)(2,1)S(1)} %maximum_bitcast_fusion), channel_id=1, source_target_pairs={{0,1},{1,2},{2,3},{3,4},{4,5},{5,6},{6,7},{7,0},{8,9},{9,10},{10,1... | collective-permute-start | bytes 196616 | tf_op jit(solution)/shard_map/ppermute | solution.py:37
  13.4 4.6 %collective-permute-start.3 = (bf16[4,8,1024]{2,0,1:T(4,128)(2,1)S(1)}, bf16[4,8,1024]{2,0,1:T(4,128)(2,1)S(1)}, u32[]{:S(2)}, u32[]{:S(2)}) collective-permute-start(bf16[4,8,1024]{2,0,1:T(4,128)(2,1)S(1)} %collective-permute-done.1), channel_id=1, source_target_pairs={{0,7},{1,0},{2,1},{3,2},{4,3},{5,4},{6,5},{7,6},{8,15},{9,8},{10,9... | collective-permute-start | bytes 196616 | tf_op jit(solution)/shard_map/ppermute | solution.py:42
  16.1 4.6 %collective-permute-start.2 = (bf16[4,8,1024]{2,0,1:T(4,128)(2,1)S(1)}, bf16[4,8,1024]{2,0,1:T(4,128)(2,1)S(1)}, u32[]{:S(2)}, u32[]{:S(2)}) collective-permute-start(bf16[4,8,1024]{2,0,1:T(4,128)(2,1)S(1)} %collective-permute-done), channel_id=1, source_target_pairs={{0,1},{1,2},{2,3},{3,4},{4,5},{5,6},{6,7},{7,0},{8,9},{9,10},{10,1... | collective-permute-start | bytes 196616 | tf_op jit(solution)/shard_map/ppermute | solution.py:37
  18.0 7.3 %collective-permute-start.5 = (bf16[4,8,1024]{2,0,1:T(4,128)(2,1)S(1)}, bf16[4,8,1024]{2,0,1:T(4,128)(2,1)S(1)}, u32[]{:S(2)}, u32[]{:S(2)}) collective-permute-start(bf16[4,8,1024]{2,0,1:T(4,128)(2,1)S(1)} %collective-permute-done.3), channel_id=1, source_target_pairs={{0,7},{1,0},{2,1},{3,2},{4,3},{5,4},{6,5},{7,6},{8,15},{9,8},{10,9... | collective-permute-start | bytes 196616 | tf_op jit(solution)/shard_map/ppermute | solution.py:42
  20.6 4.6 %collective-permute-start.4 = (bf16[4,8,1024]{2,0,1:T(4,128)(2,1)S(1)}, bf16[4,8,1024]{2,0,1:T(4,128)(2,1)S(1)}, u32[]{:S(2)}, u32[]{:S(2)}) collective-permute-start(bf16[4,8,1024]{2,0,1:T(4,128)(2,1)S(1)} %collective-permute-done.2), channel_id=1, source_target_pairs={{0,1},{1,2},{2,3},{3,4},{4,5},{5,6},{6,7},{7,0},{8,9},{9,10},{10,1... | collective-permute-start | bytes 196616 | tf_op jit(solution)/shard_map/ppermute | solution.py:37
  25.2 4.6 %collective-permute-start.6 = (bf16[4,8,1024]{2,0,1:T(4,128)(2,1)S(1)}, bf16[4,8,1024]{2,0,1:T(4,128)(2,1)S(1)}, u32[]{:S(2)}, u32[]{:S(2)}) collective-permute-start(bf16[4,8,1024]{2,0,1:T(4,128)(2,1)S(1)} %collective-permute-done.4), channel_id=1, source_target_pairs={{0,1},{1,2},{2,3},{3,4},{4,5},{5,6},{6,7},{7,0},{8,9},{9,10},{10,1... | collective-permute-start | bytes 196616 | tf_op jit(solution)/shard_map/ppermute | solution.py:37
  50.2 7.2 %slice-start = ((s8[7340032]{0:T(1024)(128)(4,1)}), s8[3145728]{0:T(1024)(128)(4,1)S(1)}, s32[]{:S(2)}) async-start(s8[7340032]{0:T(1024)(128)(4,1)} %bitcast.44), calls=%async_computation.3 | async-start | bytes 6291456
  52.1 5.3 %slice-start.1 = ((s8[7340032]{0:T(1024)(128)(4,1)}), s8[4194304]{0:T(1024)(128)(4,1)S(1)}, s32[]{:S(2)}) async-start(s8[7340032]{0:T(1024)(128)(4,1)} %bitcast.44), calls=%async_computation.4 | async-start | bytes 8388608
  52.1 7.4 %slice-start.4 = ((s8[7340032]{0:T(1024)(128)(4,1)}), s8[4194304]{0:T(1024)(128)(4,1)S(1)}, s32[]{:S(2)}) async-start(s8[7340032]{0:T(1024)(128)(4,1)} %bitcast.48), calls=%async_computation.7 | async-start | bytes 8388608
  57.4 2.1 slice-start.5
  57.4 2.1 copy-start
  62.9 0.7 copy-start.13
  63.0 167.3 %reduce-scatter.2.cloned.1.call-start = ((), (), s32[]{:S(2)}) async-start(), calls=%async_computation.1 | async-start | bytes 589824 | tf_op jit(solution)/shard_map/reduce_scatter | solution.py:85
  168.6 5.9 %copy-start.1 = (bf16[128,1024]{1,0:T(8,128)(2,1)S(1)}, bf16[128,1024]{1,0:T(8,128)(2,1)}, u32[]{:S(2)}) copy-start(bf16[128,1024]{1,0:T(8,128)(2,1)} %reshape.36) | copy-start | bytes 786436
  168.6 5.9 %copy-start.6 = (bf16[128,3584]{1,0:T(8,128)(2,1)S(1)}, bf16[128,3584]{1,0:T(8,128)(2,1)}, u32[]{:S(2)}) copy-start(bf16[128,3584]{1,0:T(8,128)(2,1)} %get-tuple-element.11) | copy-start | bytes 2752516
  168.6 5.9 %copy-start.10 = (bf16[128,3584]{1,0:T(8,128)(2,1)S(1)}, bf16[128,3584]{1,0:T(8,128)(2,1)}, u32[]{:S(2)}) copy-start(bf16[128,3584]{1,0:T(8,128)(2,1)} %get-tuple-element.13) | copy-start | bytes 2752516
  180.0 10.3 %slice-start.2 = ((s8[7340032]{0:T(1024)(128)(4,1)}), s8[3145728]{0:T(1024)(128)(4,1)S(1)}, s32[]{:S(2)}) async-start(s8[7340032]{0:T(1024)(128)(4,1)} %bitcast.46), calls=%async_computation.5 | async-start | bytes 6291456
  183.6 6.6 %slice-start.3 = ((s8[7340032]{0:T(1024)(128)(4,1)}), s8[4194304]{0:T(1024)(128)(4,1)S(1)}, s32[]{:S(2)}) async-start(s8[7340032]{0:T(1024)(128)(4,1)} %bitcast.46), calls=%async_computation.6 | async-start | bytes 8388608
  183.7 6.6 %copy-start.8 = (bf16[128,3584]{1,0:T(8,128)(2,1)S(1)}, bf16[128,3584]{1,0:T(8,128)(2,1)}, u32[]{:S(2)}) copy-start(bf16[128,3584]{1,0:T(8,128)(2,1)} %get-tuple-element.12) | copy-start | bytes 2752516
  183.7 6.6 %copy-start.11 = (bf16[128,3584]{1,0:T(8,128)(2,1)S(1)}, bf16[128,3584]{1,0:T(8,128)(2,1)}, u32[]{:S(2)}) copy-start(bf16[128,3584]{1,0:T(8,128)(2,1)} %get-tuple-element.13) | copy-start | bytes 2752516
  193.6 3.4 %copy-start.9 = (bf16[128,3584]{1,0:T(8,128)(2,1)S(1)}, bf16[128,3584]{1,0:T(8,128)(2,1)}, u32[]{:S(2)}) copy-start(bf16[128,3584]{1,0:T(8,128)(2,1)} %get-tuple-element.12) | copy-start | bytes 2752516
  193.6 3.4 %copy-start.12 = (bf16[128,3584]{1,0:T(8,128)(2,1)S(1)}, bf16[128,3584]{1,0:T(8,128)(2,1)}, u32[]{:S(2)}) copy-start(bf16[128,3584]{1,0:T(8,128)(2,1)} %get-tuple-element.13) | copy-start | bytes 2752516
  197.0 5.4 %copy-start.7 = (bf16[128,3584]{1,0:T(8,128)(2,1)S(1)}, bf16[128,3584]{1,0:T(8,128)(2,1)}, u32[]{:S(2)}) copy-start(bf16[128,3584]{1,0:T(8,128)(2,1)} %get-tuple-element.11) | copy-start | bytes 2752516
  202.4 28.8 %copy-start.2 = (bf16[4,4,1024]{2,1,0:T(4,128)(2,1)S(1)}, bf16[4,4,1024]{2,1,0:T(4,128)(2,1)}, u32[]{:S(2)}) copy-start(bf16[4,4,1024]{2,1,0:T(4,128)(2,1)} %param.7) | copy-start | bytes 98308
  202.4 68.8 %copy-start.3 = (bf16[4,4,1024]{2,1,0:T(4,128)(2,1)S(1)}, bf16[4,4,1024]{2,1,0:T(4,128)(2,1)}, u32[]{:S(2)}) copy-start(bf16[4,4,1024]{2,1,0:T(4,128)(2,1)} %param.12) | copy-start | bytes 98308
  271.0 1.5 copy-start.5
Sparse Core Ops, SparseCore 0:
  63.1 105.4 all-reduce.3
  197.1 33.1 reduce-scatter.1
